TPU v7x, 32 devices: a whole 2x2x4 slice. The times are simulated.
32 devices in a mesh: seq: 8 (over z, y), grp: 4 (over x, core).
Axes of the slice: x: 2, y: 2, z: 4, core: 2. Of those that a mesh axis runs over, the one named last changes fastest.
Arguments:
- query_rows: bfloat16 [4096, 8192], P(('seq', 'grp')), may hold values from -6 to 6
- key_matrix: bfloat16 [4096, 1024], P(('seq', 'grp')), may hold values from -6 to 6
- value_matrix: bfloat16 [4096, 1024], P(('seq', 'grp')), may hold values from -6 to 6
- vertical: int32 [64, 3], replicated, may hold values from 0 to 63, as said below
- slash_offsets: int32 [64, 3], replicated, may hold values from 0 to 8, as said below
Outputs:
- attended: bfloat16 [4096, 8192], P(('seq', 'grp'))
Inputs may be any that keep to these rules, and one draw needn't show every extreme that they name: Each head's vertical blocks are distinct and rise along the row. `slash_offsets`: column 0 is 0; each head's offsets are distinct and rise along the row.
All inputs are finite; a program needn't handle non-finite values.
Results may differ from a plain program's by a relative error of at most 0.0043.
Values may be sent and summed in bfloat16 or wider, within the bound.
No kernel may reach another device: no remote copies, remote signals or barrier semaphores. Data moves between devices by JAX's collectives and lax.ppermute only.
A program may use at most 64 MiB of HBM per device.

v0:
```python
import jax
import jax.numpy as jnp
from jax import lax
from jax.sharding import PartitionSpec as P

HEAD_DIMENSION = 128
MASK_BLOCK_SIZE = 64


def passed_along(shard, axis, by):
    length = lax.axis_size(axis)
    pairs = [(i, i + by) for i in range(length) if 0 <= i + by < length]
    return lax.ppermute(shard, axis, pairs)


def head_attention(
    query_block, slash_keys, slash_values, vert_keys, vert_values, offsets, vert_blocks, first_block
):
    block_count, block_size, head_size = query_block.shape
    vert_tiled = jnp.broadcast_to(vert_keys[None], (block_count,) + vert_keys.shape)
    vert_vtiled = jnp.broadcast_to(vert_values[None], (block_count,) + vert_values.shape)
    all_keys = jnp.concatenate([slash_keys, vert_tiled], 1).reshape(block_count, -1, head_size)
    all_values = jnp.concatenate([slash_values, vert_vtiled], 1).reshape(block_count, -1, head_size)
    scores = jnp.einsum(
        "qid,qkd->qik", query_block, all_keys, preferred_element_type=jnp.float32
    ) * head_size ** (-0.5)
    query_index = first_block + jnp.arange(block_count, dtype=jnp.int32)
    slash_block = query_index[:, None] - offsets[None, :]
    slash_good = slash_block >= 0
    vert_good = (vert_blocks[None, :] <= query_index[:, None]) & jnp.all(
        query_index[:, None, None] - vert_blocks[None, :, None] != offsets[None, None, :], axis=2
    )
    block_ids = jnp.concatenate(
        [slash_block, jnp.broadcast_to(vert_blocks[None, :], (block_count, vert_blocks.shape[0]))],
        1,
    )
    block_good = jnp.concatenate([slash_good, vert_good], 1)
    position = jnp.arange(block_size, dtype=jnp.int32)
    key_pos = (block_ids[:, :, None] * block_size + position[None, None, :]).reshape(
        block_count, -1
    )
    query_pos = query_index[:, None] * block_size + position[None, :]
    allowed = jnp.repeat(block_good, block_size, axis=1)[:, None, :] & (
        key_pos[:, None, :] <= query_pos[:, :, None]
    )
    masked = jnp.where(allowed, scores, -1e30)
    row_top = jnp.max(masked, axis=2, keepdims=True)
    weight = jnp.where(allowed, jnp.exp(masked - row_top), 0.0)
    row_total = jnp.sum(weight, axis=2, keepdims=True)
    rounded = weight.astype(jnp.bfloat16)
    result = (
        jnp.einsum("qik,qkd->qid", rounded, all_values, preferred_element_type=jnp.float32)
        / row_total
    )
    return result.astype(jnp.bfloat16)


def per_device(query_rows, key_matrix, value_matrix, vertical, slash_offsets):
    tok_rows = query_rows.shape[0]
    grp_count = lax.axis_size("grp")
    head_size = HEAD_DIMENSION
    block_size = MASK_BLOCK_SIZE
    local_heads = query_rows.shape[1] // (grp_count * head_size)
    local_kv = key_matrix.shape[1] // (grp_count * head_size)
    group_sharing_factor = local_heads // local_kv
    query_split = query_rows.reshape(tok_rows, grp_count, local_heads * head_size)
    key_split = key_matrix.reshape(tok_rows, grp_count, local_kv * head_size)
    value_split = value_matrix.reshape(tok_rows, grp_count, local_kv * head_size)
    query_group, key_group, value_group = (
        lax.all_to_all(query_split, "grp", split_axis=1, concat_axis=0, tiled=True),
        lax.all_to_all(key_split, "grp", split_axis=1, concat_axis=0, tiled=True),
        lax.all_to_all(value_split, "grp", split_axis=1, concat_axis=0, tiled=True),
    )
    group_rows = tok_rows * grp_count
    group_blocks = group_rows // block_size
    key_local = key_group.reshape(group_rows, local_kv, head_size)
    value_local = value_group.reshape(group_rows, local_kv, head_size)
    key_before, value_before = passed_along((key_local, value_local), "seq", 1)
    key_window = (
        jnp.concatenate([key_before, key_local], 0)
        .reshape(2 * group_blocks, block_size, local_kv, head_size)
        .transpose(2, 0, 1, 3)
    )
    value_window = (
        jnp.concatenate([value_before, value_local], 0)
        .reshape(2 * group_blocks, block_size, local_kv, head_size)
        .transpose(2, 0, 1, 3)
    )
    seq_index = lax.axis_index("seq")
    grp_index = lax.axis_index("grp")
    head_offsets = lax.dynamic_slice_in_dim(slash_offsets, grp_index * local_heads, local_heads, 0)
    head_verts = lax.dynamic_slice_in_dim(vertical, grp_index * local_heads, local_heads, 0)
    kv_index = jnp.arange(local_heads, dtype=jnp.int32) // group_sharing_factor
    owner_seq = head_verts // group_blocks
    local_block = head_verts % group_blocks
    key_own = key_window[:, group_blocks:]
    value_own = value_window[:, group_blocks:]
    picked_keys = key_own[kv_index[:, None], local_block]
    picked_values = value_own[kv_index[:, None], local_block]
    owned = (owner_seq == seq_index)[:, :, None, None]
    nothing = jnp.zeros((), jnp.float32)
    summed_keys, summed_values = lax.psum(
        (
            jnp.where(owned, picked_keys.astype(jnp.float32), nothing),
            jnp.where(owned, picked_values.astype(jnp.float32), nothing),
        ),
        "seq",
    )
    vert_keys = summed_keys.astype(jnp.bfloat16)
    vert_values = summed_values.astype(jnp.bfloat16)
    head_queries = (
        query_group.reshape(group_rows, local_heads, head_size)
        .transpose(1, 0, 2)
        .reshape(local_heads, group_blocks, block_size, head_size)
    )
    nearby = jnp.arange(group_blocks, dtype=jnp.int32)
    first_block = seq_index * group_blocks

    def per_head(items):
        queries_one, offsets, vert_blocks, vert_key, vert_value, kv_one = items
        window_index = group_blocks + nearby[:, None] - offsets[None, :]
        slash_keys = key_window[kv_one][window_index]
        slash_values = value_window[kv_one][window_index]
        return head_attention(
            queries_one,
            slash_keys,
            slash_values,
            vert_key,
            vert_value,
            offsets,
            vert_blocks,
            first_block,
        )

    results = lax.map(
        per_head, (head_queries, head_offsets, head_verts, vert_keys, vert_values, kv_index)
    )
    merged = (
        results.reshape(local_heads, group_rows, head_size)
        .transpose(1, 0, 2)
        .reshape(group_rows, 1, local_heads * head_size)
    )
    returned = lax.all_to_all(merged, "grp", split_axis=0, concat_axis=1, tiled=True)
    return returned.reshape(tok_rows, grp_count * local_heads * head_size)


def solution(mesh):
    return jax.shard_map(
        per_device,
        mesh=mesh,
        in_specs=(
            P(("seq", "grp"), None),
            P(("seq", "grp"), None),
            P(("seq", "grp"), None),
            P(),
            P(),
        ),
        out_specs=P(("seq", "grp"), None),
        check_vma=False,
    )
```

profile of v0, /device:TPU:0, one launch (start us, length us, event | category | flops | bytes accessed | tf_op | source)
XLA Modules:
  0.0 408.5 jit_solution(12489217705326246221)
XLA Ops:
  0.0 1.8 copy.79
  1.8 4.2 %all-to-all-start.2 = ((bf16[128,4,256]{2,0,1:T(8,128)(2,1)}), bf16[128,4,256]{2,0,1:T(8,128)(2,1)S(1)}, u32[]{:S(2)}, u32[]{:S(2)}) async-start(bf16[128,4,256]{2,0,1:T(8,128)(2,1)} %bitcast.88), calls=%async_computation.2 | async-start | bytes 524288 | tf_op jit(solution)/shard_map/all_to_all | solution.py:72
  6.3 1.7 copy.80
  8.0 4.1 all-to-all-done.2
  12.1 3.4 all-to-all-start.1
  15.6 4.1 collective-permute-start.1
  19.6 1.5 copy.78
  21.5 3.7 all-to-all-start
  25.3 4.1 collective-permute-start
  30.4 5.1 %collective-permute-done = bf16[512,2,128]{2,1,0:T(2,128)(2,1)S(1)} collective-permute-done((bf16[512,2,128]{2,1,0:T(2,128)(2,1)S(1)}, bf16[512,2,128]{2,1,0:T(2,128)(2,1)S(1)}, u32[]{:S(2)}, u32[]{:S(2)}) %collective-permute-start) | collective-permute-done | bytes 262176 | tf_op jit(solution)/shard_map/ppermute | solution.py:13
  37.3 1.8 gather_fusion.2
  39.1 1.8 gather_fusion.3
  40.9 3.3 convert_select_fusion
  44.3 128.2 %all-reduce.2 = (bf16[16,3,64,128]{3,2,1,0:T(8,128)(2,1)}, bf16[16,3,64,128]{3,2,1,0:T(8,128)(2,1)}) all-reduce(f32[16,3,64,128]{3,2,1,0:T(8,128)} %get-tuple-element.173, f32[16,3,64,128]{3,2,1,0:T(8,128)} %get-tuple-element.172), channel_id=1, replica_groups=mesh['seq'=8,'grp'=4] {'seq'}, use_global_device_ids=true, to_apply=%region_0.1 | all-reduce | flops 786432 | bytes 4718592 | tf_op jit(solution)/shard_map/psum | solution.py:102
  173.1 1.9 copy.61
  175.0 178.8 %while.11 = (s32[]{:T(128)}, bf16[16,8,64,128]{3,2,1,0:T(8,128)(2,1)}, s32[]{:T(128)}, s32[16,3]{1,0:T(8,128)S(1)}, s32[16,3]{1,0:T(8,128)S(1)}, /*index=5*/bf16...) while((s32[]{:T(128)}, ...), condition=%wide.region_6.7_spmd.clone, body=%wide.region_2.6_spmd.clone.sunk | while | flops 104339728 | bytes 11976439 | solution.py:135
  181.3 1.4 fusion.47
  184.5 1.7 fusion.49
  195.7 1.7 fusion.49
  206.9 1.7 fusion.49
  214.8 1.4 fusion.47
  218.0 1.7 fusion.49
  229.2 1.7 fusion.49
  237.2 1.4 fusion.47
  240.4 1.7 fusion.49
  248.4 1.4 fusion.47
  251.6 1.7 fusion.49
  262.7 1.7 fusion.49
  273.9 1.7 fusion.49
  281.9 1.4 fusion.47
  285.1 1.7 fusion.49
  296.3 1.7 fusion.49
  307.5 1.7 fusion.49
  315.4 1.4 fusion.47
  318.6 1.7 fusion.49
  329.8 1.7 fusion.49
  341.0 1.7 fusion.49
  349.0 1.4 fusion.47
  352.2 1.7 fusion.49
  353.8 2.9 copy.62
  357.2 2.9 reduce
  360.1 2.9 copy.81
  363.0 2.8 reshape.314
  365.8 29.3 %all_to_all.60 = bf16[4,2,131072]{2,1,0:T(2,128)(2,1)S(1)} all-to-all(bf16[4,2,131072]{2,1,0:T(2,128)(2,1)} %reshape.314), channel_id=1, replica_groups=mesh['seq'=8,'grp'=4] {'grp'}, dimensions={0} | all-to-all | bytes 4194304 | tf_op jit(solution)/shard_map/all_to_all | solution.py:143
  395.1 3.3 reshape.315
  398.4 3.5 copy.66
  401.9 2.6 copy.64
  404.4 4.1 copy.65
  (554 shorter events, 116.1 us)
Async XLA Ops:
  0.0 6.0 %copy-start = (s32[64,3]{0,1:T(4,128)S(1)}, s32[64,3]{0,1:T(4,128)}, u32[]{:S(2)}) copy-start(s32[64,3]{0,1:T(4,128)} %param.10) | copy-start | bytes 2308
  0.0 19.6 %copy-start.2 = (bf16[128,8192]{1,0:T(8,128)(2,1)S(1)}, bf16[128,8192]{1,0:T(8,128)(2,1)}, u32[]{:S(2)}) copy-start(bf16[128,8192]{1,0:T(8,128)(2,1)} %param.7) | copy-start | bytes 6291460
  1.8 10.2 %all-to-all-start.2 = ((bf16[128,4,256]{2,0,1:T(8,128)(2,1)}), bf16[128,4,256]{2,0,1:T(8,128)(2,1)S(1)}, u32[]{:S(2)}, u32[]{:S(2)}) async-start(bf16[128,4,256]{2,0,1:T(8,128)(2,1)} %bitcast.88), calls=%async_computation.2 | async-start | bytes 524288 | tf_op jit(solution)/shard_map/all_to_all | solution.py:72
  12.1 9.4 %all-to-all-start.1 = ((bf16[128,4,256]{2,0,1:T(8,128)(2,1)}), bf16[128,4,256]{2,0,1:T(8,128)(2,1)S(1)}, u32[]{:S(2)}, u32[]{:S(2)}) async-start(bf16[128,4,256]{2,0,1:T(8,128)(2,1)} %bitcast.89), calls=%async_computation.1 | async-start | bytes 524288 | tf_op jit(solution)/shard_map/all_to_all | solution.py:71
  15.6 14.2 %collective-permute-start.1 = (bf16[512,2,128]{2,1,0:T(2,128)(2,1)S(1)}, bf16[512,2,128]{2,1,0:T(2,128)(2,1)S(1)}, u32[]{:S(2)}, u32[]{:S(2)}) collective-permute-start(bf16[512,2,128]{2,1,0:T(2,128)(2,1)S(1)} %reshape.263), channel_id=1, source_target_pairs={{0,4},{4,8},{8,12},{12,16},{16,20},{20,24},{24,28},{1,5},{5,9},{9,... | collective-permute-start | bytes 786440 | tf_op jit(solution)/shard_map/ppermute | solution.py:13
  21.5 7.9 %copy-start.3 = (s32[64,3]{0,1:T(4,128)S(1)}, s32[64,3]{0,1:T(4,128)}, u32[]{:S(2)}) copy-start(s32[64,3]{0,1:T(4,128)} %param.11) | copy-start | bytes 2308
  21.5 151.0 %all-to-all-start = ((bf16[128,4,2048]{2,0,1:T(8,128)(2,1)}), bf16[128,4,2048]{2,0,1:T(8,128)(2,1)S(1)}, u32[]{:S(2)}, u32[]{:S(2)}) async-start(bf16[128,4,2048]{2,0,1:T(8,128)(2,1)} %bitcast.87), calls=%async_computation | async-start | bytes 4194304 | tf_op jit(solution)/shard_map/all_to_all | solution.py:70
  25.3 10.2 %collective-permute-start = (bf16[512,2,128]{2,1,0:T(2,128)(2,1)S(1)}, bf16[512,2,128]{2,1,0:T(2,128)(2,1)S(1)}, u32[]{:S(2)}, u32[]{:S(2)}) collective-permute-start(bf16[512,2,128]{2,1,0:T(2,128)(2,1)S(1)} %reshape.260), channel_id=1, source_target_pairs={{0,4},{4,8},{8,12},{12,16},{16,20},{20,24},{24,28},{1,5},{5,9},{9,... | collective-permute-start | bytes 786440 | tf_op jit(solution)/shard_map/ppermute | solution.py:13
  36.5 0.8 copy-start.1
where the time goes:
time: 411 us; the launch traced here: 408 us
  blocking collectives  157 us (38%)
  local copies, waits for them, and re-layouts  109 us (27%)
  matrix products  48.8 us (12%)
  other arithmetic  33 us (8%)
  loops' own time  31.1 us (8%)
  starting transfers between devices  19.5 us (5%)
  waiting for transfers between devices  9.59 us (2%)
    psum x1, blocking collectives, per_device(): lax.psum((jnp.where(owned, picked_keys.astype(jnp.float32), nothing), jnp...  128 us
    another operation x1, loops' own time, per_device(): lax.map(per_head, (head_queries, head_offsets, head_verts, vert_keys, ver...  31.1 us
    all_to_all x1, blocking collectives, per_device(): lax.all_to_all(merged, 'grp', split_axis=0, concat_axis=1, tiled=True)  29.3 us
    dot_general x16, matrix products, head_attention(): jnp.einsum('qik,qkd->qid', rounded, all_values, preferred_element_type=jn...  26.6 us
    dot_general x16, matrix products, head_attention(): jnp.einsum('qid,qkd->qik', query_block, all_keys, preferred_element_type=...  22.1 us
    squeeze x16, local copies, waits for them, and re-layouts, per_head(): slash_values = value_window[kv_one][window_index]  16.3 us
    sub x16, other arithmetic, head_attention(): weight = jnp.where(allowed, jnp.exp(masked - row_top), 0.0)  16.2 us
    unnamed x16, local copies, waits for them, and re-layouts  16 us
  transfers between devices with their start and end apart: 5, of which 3 were waited for; matrix products, arithmetic and copies ran while one was open for 3% of the time, Pallas kernels for 0%

commit v1 on v0

--- a/solution.py
+++ b/solution.py
@@ -5,6 +5,22 @@
 
 HEAD_DIMENSION = 128
 MASK_BLOCK_SIZE = 64
+
+
+def pairwise_exchange(x, axis, split, join):
+    ways, here = (lax.axis_size(axis), lax.axis_index(axis))
+    width = x.shape[split] // ways
+    shape = list(x.shape)
+    shape[split] = width
+    height = shape[join]
+    shape[join] = height * ways
+    full = jnp.zeros(shape, x.dtype)
+    for mask in range(ways):
+        part = lax.dynamic_slice_in_dim(x, (here ^ mask) * width, width, axis=split)
+        if mask:
+            part = lax.ppermute(part, axis, [(d, d ^ mask) for d in range(ways)])
+        full = lax.dynamic_update_slice_in_dim(full, part, (here ^ mask) * height, axis=join)
+    return full
 
 
 def passed_along(shard, axis, by):
@@ -140,7 +156,7 @@
         .transpose(1, 0, 2)
         .reshape(group_rows, 1, local_heads * head_size)
     )
-    returned = lax.all_to_all(merged, "grp", split_axis=0, concat_axis=1, tiled=True)
+    returned = pairwise_exchange(merged, "grp", 0, 1)
     return returned.reshape(tok_rows, grp_count * local_heads * head_size)
 
 

time: 411 us -> 395 us (0.961)
  blocking collectives: 157 us -> 128 us
  waiting for transfers between devices: 9.59 us -> 28 us
    all_to_all x1 -> x0, blocking collectives: 29.3 us -> none  [per_device(): lax.all_to_all(merged, 'grp', split_axis=0, concat_axis=1, tiled=True)]
    ppermute x0 -> x3, waiting for transfers between devices: none -> 18.4 us  [pairwise_exchange(): part = lax.ppermute(part, axis, [(d, d ^ mask) for d in range(ways)])]
    dynamic_update_slice x0 -> x4, local copies, waits for them, and re-layouts: none -> 11.5 us  [pairwise_exchange(): lax.dynamic_update_slice_in_dim(full, part, (here ^ mask) * height, axis=...]
    unnamed x16 -> x15, local copies, waits for them, and re-layouts: 16 us -> 7.53 us
    reshape x2 -> x0, local copies, waits for them, and re-layouts: 4.59 us -> none  [the longest x1 4.06 us: per_device(): return returned.reshape(tok_rows, grp_count * local_heads * head_size)]
  transfers between devices with their start and end apart: 5 -> 8, of which waited for: 3 -> 6; matrix products, arithmetic and copies ran while one was open for 3% -> 4% of each run, Pallas kernels for 0% -> 0%
where the time goes in v1:
time: 395 us; the launch traced here: 392 us
  blocking collectives  128 us (32%)
  local copies, waits for them, and re-layouts  108 us (27%)
  matrix products  48.8 us (12%)
  other arithmetic  30.1 us (8%)
  waiting for transfers between devices  28 us (7%)
  loops' own time  27.5 us (7%)
  starting transfers between devices  21.3 us (5%)
    psum x1, blocking collectives, per_device(): lax.psum((jnp.where(owned, picked_keys.astype(jnp.float32), nothing), jnp...  128 us
    another operation x1, loops' own time, per_device(): lax.map(per_head, (head_queries, head_offsets, head_verts, vert_keys, ver...  27.5 us
    dot_general x16, matrix products, head_attention(): jnp.einsum('qik,qkd->qid', rounded, all_values, preferred_element_type=jn...  26.6 us
    dot_general x16, matrix products, head_attention(): jnp.einsum('qid,qkd->qik', query_block, all_keys, preferred_element_type=...  22.1 us
    ppermute x3, waiting for transfers between devices, pairwise_exchange(): part = lax.ppermute(part, axis, [(d, d ^ mask) for d in range(ways)])  18.4 us
    squeeze x16, local copies, waits for them, and re-layouts, per_head(): slash_values = value_window[kv_one][window_index]  16.3 us
    sub x16, other arithmetic, head_attention(): weight = jnp.where(allowed, jnp.exp(masked - row_top), 0.0)  16.2 us
    broadcast_in_dim x32, local copies, waits for them, and re-layouts, head_attention(): jnp.broadcast_to(vert_values[None], (block_count,) + vert_values.shape)  14.6 us
  transfers between devices with their start and end apart: 8, of which 6 were waited for; matrix products, arithmetic and copies ran while one was open for 4% of the time, Pallas kernels for 0%

profile of v1, /device:TPU:0, one launch (start us, length us, event | category | flops | bytes accessed | tf_op | source)
XLA Modules:
  0.0 392.1 jit_solution(13412131333629569536)
XLA Ops:
  0.0 1.8 copy.65
  1.8 4.2 %all-to-all-start.2 = ((bf16[128,4,256]{2,0,1:T(8,128)(2,1)}), bf16[128,4,256]{2,0,1:T(8,128)(2,1)S(1)}, u32[]{:S(2)}, u32[]{:S(2)}) async-start(bf16[128,4,256]{2,0,1:T(8,128)(2,1)} %bitcast.86), calls=%async_computation.2 | async-start | bytes 524288 | tf_op jit(solution)/shard_map/all_to_all | solution.py:88
  6.3 1.7 copy.66
  8.0 4.1 %all-to-all-done.2 = bf16[128,4,256]{2,0,1:T(8,128)(2,1)S(1)} async-done(((bf16[128,4,256]{2,0,1:T(8,128)(2,1)}), bf16[128,4,256]{2,0,1:T(8,128)(2,1)S(1)}, u32[]{:S(2)}, u32[]{:S(2)}) %all-to-all-start.2) | async-done | bytes 262176 | tf_op jit(solution)/shard_map/all_to_all | solution.py:88
  12.1 3.4 all-to-all-start.1
  15.6 4.1 %collective-permute-start.1 = (bf16[512,2,128]{2,1,0:T(2,128)(2,1)S(1)}, bf16[512,2,128]{2,1,0:T(2,128)(2,1)S(1)}, u32[]{:S(2)}, u32[]{:S(2)}) collective-permute-start(bf16[512,2,128]{2,1,0:T(2,128)(2,1)S(1)} %reshape.262), channel_id=1, source_target_pairs={{0,4},{4,8},{8,12},{12,16},{16,20},{20,24},{24,28},{1,5},{5,9},{9,... | collective-permute-start | bytes 786440 | tf_op jit(solution)/shard_map/ppermute | solution.py:29
  19.6 1.5 copy.64
  21.5 3.7 all-to-all-start
  25.3 4.1 %collective-permute-start = (bf16[512,2,128]{2,1,0:T(2,128)(2,1)S(1)}, bf16[512,2,128]{2,1,0:T(2,128)(2,1)S(1)}, u32[]{:S(2)}, u32[]{:S(2)}) collective-permute-start(bf16[512,2,128]{2,1,0:T(2,128)(2,1)S(1)} %reshape.259), channel_id=1, source_target_pairs={{0,4},{4,8},{8,12},{12,16},{16,20},{20,24},{24,28},{1,5},{5,9},{9,... | collective-permute-start | bytes 786440 | tf_op jit(solution)/shard_map/ppermute | solution.py:29
  30.4 5.1 %collective-permute-done = bf16[512,2,128]{2,1,0:T(2,128)(2,1)S(1)} collective-permute-done((bf16[512,2,128]{2,1,0:T(2,128)(2,1)S(1)}, bf16[512,2,128]{2,1,0:T(2,128)(2,1)S(1)}, u32[]{:S(2)}, u32[]{:S(2)}) %collective-permute-start) | collective-permute-done | bytes 262176 | tf_op jit(solution)/shard_map/ppermute | solution.py:29
  37.3 1.8 gather_fusion.2
  39.1 1.8 gather_fusion.3
  40.9 3.3 convert_select_fusion
  44.2 128.2 %all-reduce.2 = (bf16[16,3,64,128]{3,2,1,0:T(8,128)(2,1)}, bf16[16,3,64,128]{3,2,1,0:T(8,128)(2,1)}) all-reduce(f32[16,3,64,128]{3,2,1,0:T(8,128)} %get-tuple-element.166, f32[16,3,64,128]{3,2,1,0:T(8,128)} %get-tuple-element.165), channel_id=1, replica_groups=mesh['seq'=8,'grp'=4] {'seq'}, use_global_device_ids=true, to_apply=%region_0.1 | all-reduce | flops 786432 | bytes 4718592 | tf_op jit(solution)/shard_map/psum | solution.py:118
  173.1 1.9 copy.48
  175.0 174.6 %while.11 = (s32[]{:T(128)}, bf16[16,8,64,128]{3,2,1,0:T(8,128)(2,1)}, s32[]{:T(128)}, s32[16,3]{1,0:T(8,128)S(1)}, s32[16,3]{1,0:T(8,128)S(1)}, /*index=5*/bf16...) while((s32[]{:T(128)}, ...), condition=%wide.region_6.7_spmd.clone, body=%wide.region_2.6_spmd.clone.sunk | while | flops 104339728 | bytes 11976439 | solution.py:151
  184.2 1.7 fusion.49
  191.9 1.4 fusion.47
  195.1 1.7 fusion.49
  202.8 1.4 fusion.47
  206.0 1.7 fusion.49
  213.8 1.4 fusion.47
  217.0 1.7 fusion.49
  227.9 1.7 fusion.49
  235.6 1.4 fusion.47
  238.8 1.7 fusion.49
  249.7 1.7 fusion.49
  257.4 1.4 fusion.47
  260.6 1.7 fusion.49
  271.5 1.7 fusion.49
  279.2 1.4 fusion.47
  282.4 1.7 fusion.49
  293.3 1.7 fusion.49
  301.0 1.4 fusion.47
  304.2 1.7 fusion.49
  315.1 1.7 fusion.49
  322.8 1.4 fusion.47
  326.1 1.7 fusion.49
  337.0 1.7 fusion.49
  344.7 1.4 fusion.47
  347.9 1.7 fusion.49
  349.5 2.9 copy.49
  358.1 11.8 %collective-permute-done.3 = bf16[128,1,2048]{0,2,1:T(8,128)(2,1)S(1)} collective-permute-done((bf16[128,1,2048]{0,2,1:T(8,128)(2,1)S(1)}, bf16[128,1,2048]{0,2,1:T(8,128)(2,1)S(1)}, u32[]{:S(2)}, u32[]{:S(2)}) %collective-permute-start.3) | collective-permute-done | bytes 524320 | tf_op jit(solution)/shard_map/ppermute | solution.py:21
  370.7 3.4 copy.50
  374.2 6.3 %collective-permute-done.4 = bf16[128,1,2048]{0,2,1:T(8,128)(2,1)} collective-permute-done((bf16[128,1,2048]{0,2,1:T(8,128)(2,1)S(1)}, bf16[128,1,2048]{0,2,1:T(8,128)(2,1)}, u32[]{:S(2)}, u32[]{:S(2)}) %collective-permute-start.4) | collective-permute-done | bytes 524320 | tf_op jit(solution)/shard_map/ppermute | solution.py:21
  380.5 2.5 copy.51
  383.0 6.4 %dynamic_update_slice.19 = bf16[128,4,2048]{2,1,0:T(4,128)(2,1)S(1)} dynamic-update-slice(bf16[128,4,2048]{2,1,0:T(4,128)(2,1)S(1)} %copy.50, bf16[128,1,2048]{2,1,0:T(2,128)(2,1)S(1)} %copy.51, s32[]{:T(128)} %constant.94.clone.1, s32[]{:T(128)S(6)} %select_n.108, s32[]{:T(128)} %constant.94.clone.1) | dynamic-update-slice | bytes 1048580 | tf_op jit(solution)/shard_map/dynamic_update_slice | solution.py:22
  389.4 2.7 copy.58
  (561 shorter events, 118.6 us)
Async XLA Ops:
  0.0 6.0 %copy-start = (s32[64,3]{0,1:T(4,128)S(1)}, s32[64,3]{0,1:T(4,128)}, u32[]{:S(2)}) copy-start(s32[64,3]{0,1:T(4,128)} %param.10) | copy-start | bytes 2308
  0.0 19.6 %copy-start.3 = (bf16[128,8192]{1,0:T(8,128)(2,1)S(1)}, bf16[128,8192]{1,0:T(8,128)(2,1)}, u32[]{:S(2)}) copy-start(bf16[128,8192]{1,0:T(8,128)(2,1)} %param.7) | copy-start | bytes 6291460
  1.8 10.2 %all-to-all-start.2 = ((bf16[128,4,256]{2,0,1:T(8,128)(2,1)}), bf16[128,4,256]{2,0,1:T(8,128)(2,1)S(1)}, u32[]{:S(2)}, u32[]{:S(2)}) async-start(bf16[128,4,256]{2,0,1:T(8,128)(2,1)} %bitcast.86), calls=%async_computation.2 | async-start | bytes 524288 | tf_op jit(solution)/shard_map/all_to_all | solution.py:88
  12.1 9.4 %all-to-all-start.1 = ((bf16[128,4,256]{2,0,1:T(8,128)(2,1)}), bf16[128,4,256]{2,0,1:T(8,128)(2,1)S(1)}, u32[]{:S(2)}, u32[]{:S(2)}) async-start(bf16[128,4,256]{2,0,1:T(8,128)(2,1)} %bitcast.87), calls=%async_computation.1 | async-start | bytes 524288 | tf_op jit(solution)/shard_map/all_to_all | solution.py:87
  15.6 14.2 %collective-permute-start.1 = (bf16[512,2,128]{2,1,0:T(2,128)(2,1)S(1)}, bf16[512,2,128]{2,1,0:T(2,128)(2,1)S(1)}, u32[]{:S(2)}, u32[]{:S(2)}) collective-permute-start(bf16[512,2,128]{2,1,0:T(2,128)(2,1)S(1)} %reshape.262), channel_id=1, source_target_pairs={{0,4},{4,8},{8,12},{12,16},{16,20},{20,24},{24,28},{1,5},{5,9},{9,... | collective-permute-start | bytes 786440 | tf_op jit(solution)/shard_map/ppermute | solution.py:29
  21.5 7.9 %copy-start.4 = (s32[64,3]{0,1:T(4,128)S(1)}, s32[64,3]{0,1:T(4,128)}, u32[]{:S(2)}) copy-start(s32[64,3]{0,1:T(4,128)} %param.11) | copy-start | bytes 2308
  21.5 151.0 %all-to-all-start = ((bf16[128,4,2048]{2,0,1:T(8,128)(2,1)}), bf16[128,4,2048]{2,0,1:T(8,128)(2,1)S(1)}, u32[]{:S(2)}, u32[]{:S(2)}) async-start(bf16[128,4,2048]{2,0,1:T(8,128)(2,1)} %bitcast.85), calls=%async_computation | async-start | bytes 4194304 | tf_op jit(solution)/shard_map/all_to_all | solution.py:86
  25.3 10.2 %collective-permute-start = (bf16[512,2,128]{2,1,0:T(2,128)(2,1)S(1)}, bf16[512,2,128]{2,1,0:T(2,128)(2,1)S(1)}, u32[]{:S(2)}, u32[]{:S(2)}) collective-permute-start(bf16[512,2,128]{2,1,0:T(2,128)(2,1)S(1)} %reshape.259), channel_id=1, source_target_pairs={{0,4},{4,8},{8,12},{12,16},{16,20},{20,24},{24,28},{1,5},{5,9},{9,... | collective-permute-start | bytes 786440 | tf_op jit(solution)/shard_map/ppermute | solution.py:29
  36.5 0.8 copy-start.2
  353.9 1.3 copy-start.1
  355.2 2.1 collective-permute-start.2
  355.2 14.7 %collective-permute-start.3 = (bf16[128,1,2048]{0,2,1:T(8,128)(2,1)S(1)}, bf16[128,1,2048]{0,2,1:T(8,128)(2,1)S(1)}, u32[]{:S(2)}, u32[]{:S(2)}) collective-permute-start(bf16[128,1,2048]{0,2,1:T(8,128)(2,1)S(1)} %get-tuple-element.162), channel_id=1, source_target_pairs={{0,2},{1,3},{2,0},{3,1},{4,6},{5,7},{6,4},{7,5},{8,10},{9,11},{10,... | collective-permute-start | bytes 1572872 | tf_op jit(solution)/shard_map/ppermute | solution.py:21
  356.4 24.0 %collective-permute-start.4 = (bf16[128,1,2048]{0,2,1:T(8,128)(2,1)S(1)}, bf16[128,1,2048]{0,2,1:T(8,128)(2,1)}, u32[]{:S(2)}, u32[]{:S(2)}) collective-permute-start(bf16[128,1,2048]{0,2,1:T(8,128)(2,1)S(1)} %get-tuple-element.161), channel_id=1, source_target_pairs={{0,3},{1,2},{2,1},{3,0},{4,7},{5,6},{6,5},{7,4},{8,11},{9,10},{10,... | collective-permute-start | bytes 1572872 | tf_op jit(solution)/shard_map/ppermute | solution.py:21
